TPU v7x, 512 devices: a whole 4x8x8 slice. The times are simulated.
512 devices in a mesh: rep: 32 (over y, z_lo, core), row: 16 (over z_hi, x).
Axes of the slice: x: 4, y: 8, z: 8 (z_hi: 4, z_lo: 2; z = z_hi * 2 + z_lo), core: 2. Of those that a mesh axis runs over, the one named last changes fastest.
Arguments:
- features: bfloat16 [65536, 128], P(('rep', 'row')), may hold values from -6 to 6
- weight: bfloat16 [128, 256], replicated, may hold values from -0.5 to 0.5
- cotangent: bfloat16 [65536, 256], P(('rep', 'row')), may hold values from -6 to 6
- tile_values: bfloat16 [32, 16, 128, 128, 128], P('rep', 'row'), may hold values from -0.046875 to 0.046875
- tile_coords: int32 [32, 16, 128, 2], P('rep', 'row'), may hold values from 0 to 31, as said below
- tile_count: int32 [32, 16], P('rep', 'row'), may hold values from 32 to 128, as said below
Outputs:
- activated: bfloat16 [65536, 256], P(('rep', 'row'))
- feature_grad: bfloat16 [65536, 128], P(('rep', 'row'))
- weight_grad: float32 [128, 256], replicated
Inputs may be any that keep to these rules, and one draw needn't show every extreme that they name: `tile_coords`: in each device's list the slots name distinct pairs; the first entry is a row tile below 32, the second a column tile below 16. `tile_count`: some device uses all 128 slots.
All inputs are finite; a program needn't handle non-finite values.
Results may differ from a plain program's by a relative error of at most 0.006.
Values may be sent and summed in bfloat16 or wider, within the bound.
No kernel may reach another device: no remote copies, remote signals or barrier semaphores. Data moves between devices by JAX's collectives and lax.ppermute only.
A program may use at most 64 MiB of HBM per device.

v0:
```python
import math

import jax
import jax.numpy as jnp
from jax import lax
from jax.sharding import PartitionSpec as P


def from_behind(block, axis, distance):
    devices = range(lax.axis_size(axis))
    route = [((i - distance) % len(devices), i) for i in devices]
    return lax.ppermute(block, axis, route)


def silu_slope(preactivation):
    sigmoid_value = jax.nn.sigmoid(preactivation)
    return sigmoid_value * (1.0 + preactivation * (1.0 - sigmoid_value))


def tile_products(values, coords, live_count, sources, buckets, adjoint):
    slot_total = values.shape[0]
    tile_size = values.shape[1]
    width = sources.shape[2]
    group_size = math.gcd(slot_total, 32)
    round_total = (live_count + group_size - 1) // group_size
    bucket_ids = jnp.arange(buckets, dtype=jnp.int32)
    pick_column = 0 if adjoint else 1
    sum_column = 1 if adjoint else 0
    form = "tji,tjf->tif" if adjoint else "tij,tjf->tif"

    def advance(turn_index, running):
        begin_at = turn_index * group_size
        tile_block = lax.dynamic_slice_in_dim(values, begin_at, group_size, 0)
        coord_block = lax.dynamic_slice_in_dim(coords, begin_at, group_size, 0)
        live_mask = begin_at + jnp.arange(group_size, dtype=jnp.int32) < live_count
        picked = jnp.take(sources, coord_block[:, pick_column], axis=0)
        product = jnp.einsum(form, tile_block, picked, preferred_element_type=jnp.float32)
        select = (
            (coord_block[:, sum_column][None, :] == bucket_ids[:, None]) & live_mask[None, :]
        ).astype(jnp.float32)
        return running + jnp.einsum("rt,tif->rif", select, product, precision=lax.Precision.HIGHEST)

    start_sum = jnp.zeros((buckets, tile_size, width), jnp.float32)
    return lax.fori_loop(0, round_total, advance, start_sum)


def local(features, weight, cotangent, tile_values, tile_coords, tile_count):
    rep_count = lax.axis_size("rep")
    row_count = lax.axis_size("row")
    tile_size = features.shape[0]
    feature_size = features.shape[1]
    values = tile_values[0, 0]
    coords = tile_coords[0, 0]
    live_count = tile_count[0, 0]
    columns = lax.all_gather(features, "row", axis=0, tiled=True).reshape(
        row_count, tile_size, feature_size
    )
    partial_rows = tile_products(values, coords, live_count, columns, rep_count, False)
    partial_rows = partial_rows.reshape(rep_count * tile_size, feature_size)
    aggregated = lax.psum_scatter(partial_rows, "rep", scatter_dimension=0, tiled=True).astype(
        jnp.bfloat16
    )
    preactivation = jnp.dot(aggregated, weight, preferred_element_type=jnp.float32)
    grad_pre = (cotangent.astype(jnp.float32) * silu_slope(preactivation)).astype(jnp.bfloat16)
    grad_hidden = lax.dot_general(
        grad_pre, weight, (((1,), (1,)), ((), ())), preferred_element_type=jnp.float32
    ).astype(jnp.bfloat16)
    grad_rows = lax.all_gather(grad_hidden, "rep", axis=0, tiled=True)
    activated = jax.nn.silu(preactivation).astype(jnp.bfloat16)
    grad_blocks = grad_rows.reshape(rep_count, tile_size, feature_size)
    back_terms = tile_products(values, coords, live_count, grad_blocks, row_count, True)
    row_place = lax.axis_index("row")

    def pass_on(turn_index, carried):
        carried = from_behind(carried, "row", 1)
        target = (row_place + row_count - 1 - turn_index) % row_count
        return carried + lax.dynamic_index_in_dim(back_terms, target, 0, keepdims=False)

    initial = lax.dynamic_index_in_dim(
        back_terms, (row_place + row_count - 1) % row_count, 0, keepdims=False
    )
    feature_sum = lax.fori_loop(1, row_count, pass_on, initial)
    feature_grad = feature_sum.astype(jnp.bfloat16)
    weight_term = lax.dot_general(
        aggregated, grad_pre, (((0,), (0,)), ((), ())), preferred_element_type=jnp.float32
    )
    weight_grad = lax.psum(weight_term, ("rep", "row"))
    return (activated, feature_grad, weight_grad)


def solution(mesh):
    placed = (
        P(("rep", "row"), None),
        P(),
        P(("rep", "row"), None),
        P("rep", "row", None, None, None),
        P("rep", "row", None, None),
        P("rep", "row"),
    )
    return jax.shard_map(
        local,
        mesh=mesh,
        in_specs=placed,
        out_specs=(P(("rep", "row"), None), P(("rep", "row"), None), P()),
        check_vma=False,
    )
```

profile of v0, /device:TPU:1, one launch (start us, length us, event | category | flops | bytes accessed | tf_op | source)
XLA Modules:
  0.0 559.5 jit_solution(3523628455512003771)
XLA Ops:
  7.9 48.6 %all_gather.6 = bf16[2048,128]{1,0:T(8,128)(2,1)} all-gather(bf16[128,128]{1,0:T(8,128)(2,1)} %param.12), channel_id=1, replica_groups=mesh['rep'=32,'row'=16] {'row'}, dimensions={0}, use_global_device_ids=true | all-gather | bytes 557056 | tf_op jit(solution)/shard_map/all_gather | solution.py:55
  56.8 29.9 %while.38 = (s32[]{:T(128)}, f32[32,128,128]{2,0,1:T(8,128)S(1)}, s32[]{:T(128)}, s32[128,2]{0,1:T(2,128)S(1)}, s32[]{:T(128)}, /*index=5*/bf16[128,128,128]{2,1...) while((s32[]{:T(128)}, f32[32,128,128]{2,0,1:T(8,128)S(1)}, ...), condition=%wide.region_1.2_spmd.clone, body=%wide.region_0.1_spmd.clone.sunk | while | flops 336596320 | bytes 12588843 | solution.py:44
  61.1 3.1 fusion.65
  68.6 3.1 fusion.65
  76.1 3.1 fusion.65
  83.5 3.1 fusion.65
  86.7 2.5 copy.10
  89.3 121.1 %reduce-scatter.2.cloned.1.call-done = f32[128,128]{1,0:T(8,128)} async-done(((f32[4096,128]{1,0:T(8,128)}), f32[128,128]{1,0:T(8,128)}) %reduce-scatter.2.cloned.1.call-update) | async-done | bytes 65552 | tf_op jit(solution)/shard_map/reduce_scatter | solution.py:60
  214.7 65.7 %all-gather.2.cloned.1.call-done = bf16[4096,128]{1,0:T(8,128)(2,1)} async-done(((bf16[128,128]{1,0:T(8,128)(2,1)}), bf16[4096,128]{1,0:T(8,128)(2,1)}) %all-gather.2.cloned.1.call-update) | async-done | bytes 1048592 | tf_op jit(solution)/shard_map/all_gather | solution.py:68
  280.5 27.4 %while.39 = (s32[]{:T(128)}, f32[16,128,128]{2,0,1:T(8,128)S(1)}, s32[]{:T(128)}, s32[128,2]{0,1:T(2,128)S(1)}, s32[]{:T(128)}, /*index=5*/bf16[128,128,128]{2,1...) while((s32[]{:T(128)}, f32[16,128,128]{2,0,1:T(8,128)S(1)}, ...), condition=%wide.region_4.5_spmd.clone, body=%wide.region_3.4_spmd.clone.sunk | while | flops 235669856 | bytes 10491691 | solution.py:44
  280.6 2.0 gather_fusion.1
  285.1 2.3 fusion.71
  287.5 2.0 gather_fusion.1
  291.9 2.3 fusion.71
  294.3 2.0 gather_fusion.1
  298.8 2.3 fusion.71
  301.1 2.0 gather_fusion.1
  305.6 2.3 fusion.71
  308.0 145.7 %while.37 = (s32[]{:T(128)}, f32[128,128]{1,0:T(8,128)S(1)}, s32[]{:T(128)}, f32[16,128,128]{2,0,1:T(8,128)S(1)}, s32[]{:T(128)}, /*index=5*/s32[]{:T(128)}, s32[]{:T(128)}, s32[]{:T(128)}) while((s32[]{:T(128)}, f32[128,128]{1,0:T(8,128)S(1)}, s32[]{:T(128)}, f32[16,128,128]{2,0,1:T(8,128)S(1)}, s32[]{:T(128)}, /*index=5*/s32[]{:T(128)}, ...), condition=%wide.region_6.7_spmd, body=%wide.region_5.6_spmd.sunk | while | flops 16401 | bytes 590108 | solution.py:82
  308.0 1.9 collective-permute-start
  310.0 7.3 %collective-permute-done = f32[128,128]{1,0:T(8,128)S(1)} collective-permute-done((f32[128,128]{1,0:T(8,128)S(1)}, f32[128,128]{1,0:T(8,128)S(1)}, u32[]{:S(2)}, u32[]{:S(2)}) %collective-permute-start) | collective-permute-done | bytes 65568 | tf_op jit(solution)/shard_map/while/body/eval_jaxpr/ppermute | solution.py:12
  317.3 1.9 collective-permute-start
  319.3 7.3 %collective-permute-done = f32[128,128]{1,0:T(8,128)S(1)} collective-permute-done((f32[128,128]{1,0:T(8,128)S(1)}, f32[128,128]{1,0:T(8,128)S(1)}, u32[]{:S(2)}, u32[]{:S(2)}) %collective-permute-start) | collective-permute-done | bytes 65568 | tf_op jit(solution)/shard_map/while/body/eval_jaxpr/ppermute | solution.py:12
  326.6 1.9 collective-permute-start
  328.7 8.2 %collective-permute-done = f32[128,128]{1,0:T(8,128)S(1)} collective-permute-done((f32[128,128]{1,0:T(8,128)S(1)}, f32[128,128]{1,0:T(8,128)S(1)}, u32[]{:S(2)}, u32[]{:S(2)}) %collective-permute-start) | collective-permute-done | bytes 65568 | tf_op jit(solution)/shard_map/while/body/eval_jaxpr/ppermute | solution.py:12
  336.9 1.9 collective-permute-start
  338.9 7.8 %collective-permute-done = f32[128,128]{1,0:T(8,128)S(1)} collective-permute-done((f32[128,128]{1,0:T(8,128)S(1)}, f32[128,128]{1,0:T(8,128)S(1)}, u32[]{:S(2)}, u32[]{:S(2)}) %collective-permute-start) | collective-permute-done | bytes 65568 | tf_op jit(solution)/shard_map/while/body/eval_jaxpr/ppermute | solution.py:12
  346.8 1.9 collective-permute-start
  348.8 7.8 %collective-permute-done = f32[128,128]{1,0:T(8,128)S(1)} collective-permute-done((f32[128,128]{1,0:T(8,128)S(1)}, f32[128,128]{1,0:T(8,128)S(1)}, u32[]{:S(2)}, u32[]{:S(2)}) %collective-permute-start) | collective-permute-done | bytes 65568 | tf_op jit(solution)/shard_map/while/body/eval_jaxpr/ppermute | solution.py:12
  356.6 1.9 collective-permute-start
  358.6 7.6 %collective-permute-done = f32[128,128]{1,0:T(8,128)S(1)} collective-permute-done((f32[128,128]{1,0:T(8,128)S(1)}, f32[128,128]{1,0:T(8,128)S(1)}, u32[]{:S(2)}, u32[]{:S(2)}) %collective-permute-start) | collective-permute-done | bytes 65568 | tf_op jit(solution)/shard_map/while/body/eval_jaxpr/ppermute | solution.py:12
  366.2 1.9 collective-permute-start
  368.2 7.8 %collective-permute-done = f32[128,128]{1,0:T(8,128)S(1)} collective-permute-done((f32[128,128]{1,0:T(8,128)S(1)}, f32[128,128]{1,0:T(8,128)S(1)}, u32[]{:S(2)}, u32[]{:S(2)}) %collective-permute-start) | collective-permute-done | bytes 65568 | tf_op jit(solution)/shard_map/while/body/eval_jaxpr/ppermute | solution.py:12
  376.1 1.9 collective-permute-start
  378.1 7.3 %collective-permute-done = f32[128,128]{1,0:T(8,128)S(1)} collective-permute-done((f32[128,128]{1,0:T(8,128)S(1)}, f32[128,128]{1,0:T(8,128)S(1)}, u32[]{:S(2)}, u32[]{:S(2)}) %collective-permute-start) | collective-permute-done | bytes 65568 | tf_op jit(solution)/shard_map/while/body/eval_jaxpr/ppermute | solution.py:12
  385.4 1.9 collective-permute-start
  387.4 8.5 %collective-permute-done = f32[128,128]{1,0:T(8,128)S(1)} collective-permute-done((f32[128,128]{1,0:T(8,128)S(1)}, f32[128,128]{1,0:T(8,128)S(1)}, u32[]{:S(2)}, u32[]{:S(2)}) %collective-permute-start) | collective-permute-done | bytes 65568 | tf_op jit(solution)/shard_map/while/body/eval_jaxpr/ppermute | solution.py:12
  396.0 1.9 collective-permute-start
  398.0 7.5 %collective-permute-done = f32[128,128]{1,0:T(8,128)S(1)} collective-permute-done((f32[128,128]{1,0:T(8,128)S(1)}, f32[128,128]{1,0:T(8,128)S(1)}, u32[]{:S(2)}, u32[]{:S(2)}) %collective-permute-start) | collective-permute-done | bytes 65568 | tf_op jit(solution)/shard_map/while/body/eval_jaxpr/ppermute | solution.py:12
  405.5 1.9 collective-permute-start
  407.5 8.2 %collective-permute-done = f32[128,128]{1,0:T(8,128)S(1)} collective-permute-done((f32[128,128]{1,0:T(8,128)S(1)}, f32[128,128]{1,0:T(8,128)S(1)}, u32[]{:S(2)}, u32[]{:S(2)}) %collective-permute-start) | collective-permute-done | bytes 65568 | tf_op jit(solution)/shard_map/while/body/eval_jaxpr/ppermute | solution.py:12
  415.8 1.9 collective-permute-start
  417.8 8.1 %collective-permute-done = f32[128,128]{1,0:T(8,128)S(1)} collective-permute-done((f32[128,128]{1,0:T(8,128)S(1)}, f32[128,128]{1,0:T(8,128)S(1)}, u32[]{:S(2)}, u32[]{:S(2)}) %collective-permute-start) | collective-permute-done | bytes 65568 | tf_op jit(solution)/shard_map/while/body/eval_jaxpr/ppermute | solution.py:12
  427.9 7.2 %collective-permute-done = f32[128,128]{1,0:T(8,128)S(1)} collective-permute-done((f32[128,128]{1,0:T(8,128)S(1)}, f32[128,128]{1,0:T(8,128)S(1)}, u32[]{:S(2)}, u32[]{:S(2)}) %collective-permute-start) | collective-permute-done | bytes 65568 | tf_op jit(solution)/shard_map/while/body/eval_jaxpr/ppermute | solution.py:12
  437.2 7.2 %collective-permute-done = f32[128,128]{1,0:T(8,128)S(1)} collective-permute-done((f32[128,128]{1,0:T(8,128)S(1)}, f32[128,128]{1,0:T(8,128)S(1)}, u32[]{:S(2)}, u32[]{:S(2)}) %collective-permute-start) | collective-permute-done | bytes 65568 | tf_op jit(solution)/shard_map/while/body/eval_jaxpr/ppermute | solution.py:12
  444.4 1.9 collective-permute-start
  446.4 7.2 %collective-permute-done = f32[128,128]{1,0:T(8,128)S(1)} collective-permute-done((f32[128,128]{1,0:T(8,128)S(1)}, f32[128,128]{1,0:T(8,128)S(1)}, u32[]{:S(2)}, u32[]{:S(2)}) %collective-permute-start) | collective-permute-done | bytes 65568 | tf_op jit(solution)/shard_map/while/body/eval_jaxpr/ppermute | solution.py:12
  454.3 97.1 %all-reduce.2.cloned.1.call-done = f32[128,256]{1,0:T(8,128)} async-done(((f32[128,256]{1,0:T(8,128)}), f32[128,256]{1,0:T(8,128)}) %all-reduce.2.cloned.1.call-update) | async-done | bytes 131088 | tf_op jit(solution)/shard_map/psum | solution.py:87
  (104 shorter events, 39.0 us)
Async XLA Ops:
  7.2 203.2 %copy-start = (bf16[128,256]{1,0:T(8,128)(2,1)S(1)}, bf16[128,256]{1,0:T(8,128)(2,1)}, u32[]{:S(2)}) copy-start(bf16[128,256]{1,0:T(8,128)(2,1)} %param.13) | copy-start | bytes 196612
  7.2 49.6 %copy-start.1 = (s32[1,1,128,2]{2,3,1,0:T(2,128)S(1)}, s32[1,1,128,2]{2,3,1,0:T(2,128)}, u32[]{:S(2)}) copy-start(s32[1,1,128,2]{2,3,1,0:T(2,128)} %param.16) | copy-start | bytes 3076
  7.2 203.2 %reduce-scatter.2.cloned.1.call-start = ((), (), s32[]{:S(2)}) async-start(), calls=%async_computation.1 | async-start | bytes 2162688 | tf_op jit(solution)/shard_map/reduce_scatter | solution.py:60
  89.2 121.2 %copy-start.2 = (bf16[128,256]{1,0:T(8,128)(2,1)S(1)}, bf16[128,256]{1,0:T(8,128)(2,1)}, u32[]{:S(2)}) copy-start(bf16[128,256]{1,0:T(8,128)(2,1)} %param.14) | copy-start | bytes 196612
  89.3 191.1 %all-gather.2.cloned.1.call-start = ((), (), s32[]{:S(2)}) async-start(), calls=%async_computation.2 | async-start | bytes 1081344 | tf_op jit(solution)/shard_map/all_gather | solution.py:68
  212.9 338.5 %all-reduce.2.cloned.1.call-start = ((), (), s32[]{:S(2)}) async-start(), calls=%async_computation.3 | async-start | bytes 262144 | tf_op jit(solution)/shard_map/psum | solution.py:87
  308.0 9.3 %collective-permute-start = (f32[128,128]{1,0:T(8,128)S(1)}, f32[128,128]{1,0:T(8,128)S(1)}, u32[]{:S(2)}, u32[]{:S(2)}) collective-permute-start(f32[128,128]{1,0:T(8,128)S(1)} %get-tuple-element.487), channel_id=1, source_target_pairs={{15,0},{0,1},{1,2},{2,3},{3,4},{4,5},{5,6},{6,7},{7,8},{8,9},{9,10... | collective-permute-start | bytes 196616 | tf_op jit(solution)/shard_map/while/body/eval_jaxpr/ppermute | solution.py:12
  317.3 9.3 %collective-permute-start = (f32[128,128]{1,0:T(8,128)S(1)}, f32[128,128]{1,0:T(8,128)S(1)}, u32[]{:S(2)}, u32[]{:S(2)}) collective-permute-start(f32[128,128]{1,0:T(8,128)S(1)} %get-tuple-element.487), channel_id=1, source_target_pairs={{15,0},{0,1},{1,2},{2,3},{3,4},{4,5},{5,6},{6,7},{7,8},{8,9},{9,10... | collective-permute-start | bytes 196616 | tf_op jit(solution)/shard_map/while/body/eval_jaxpr/ppermute | solution.py:12
  326.6 10.2 %collective-permute-start = (f32[128,128]{1,0:T(8,128)S(1)}, f32[128,128]{1,0:T(8,128)S(1)}, u32[]{:S(2)}, u32[]{:S(2)}) collective-permute-start(f32[128,128]{1,0:T(8,128)S(1)} %get-tuple-element.487), channel_id=1, source_target_pairs={{15,0},{0,1},{1,2},{2,3},{3,4},{4,5},{5,6},{6,7},{7,8},{8,9},{9,10... | collective-permute-start | bytes 196616 | tf_op jit(solution)/shard_map/while/body/eval_jaxpr/ppermute | solution.py:12
  336.9 9.9 %collective-permute-start = (f32[128,128]{1,0:T(8,128)S(1)}, f32[128,128]{1,0:T(8,128)S(1)}, u32[]{:S(2)}, u32[]{:S(2)}) collective-permute-start(f32[128,128]{1,0:T(8,128)S(1)} %get-tuple-element.487), channel_id=1, source_target_pairs={{15,0},{0,1},{1,2},{2,3},{3,4},{4,5},{5,6},{6,7},{7,8},{8,9},{9,10... | collective-permute-start | bytes 196616 | tf_op jit(solution)/shard_map/while/body/eval_jaxpr/ppermute | solution.py:12
  346.8 9.8 %collective-permute-start = (f32[128,128]{1,0:T(8,128)S(1)}, f32[128,128]{1,0:T(8,128)S(1)}, u32[]{:S(2)}, u32[]{:S(2)}) collective-permute-start(f32[128,128]{1,0:T(8,128)S(1)} %get-tuple-element.487), channel_id=1, source_target_pairs={{15,0},{0,1},{1,2},{2,3},{3,4},{4,5},{5,6},{6,7},{7,8},{8,9},{9,10... | collective-permute-start | bytes 196616 | tf_op jit(solution)/shard_map/while/body/eval_jaxpr/ppermute | solution.py:12
  356.6 9.6 %collective-permute-start = (f32[128,128]{1,0:T(8,128)S(1)}, f32[128,128]{1,0:T(8,128)S(1)}, u32[]{:S(2)}, u32[]{:S(2)}) collective-permute-start(f32[128,128]{1,0:T(8,128)S(1)} %get-tuple-element.487), channel_id=1, source_target_pairs={{15,0},{0,1},{1,2},{2,3},{3,4},{4,5},{5,6},{6,7},{7,8},{8,9},{9,10... | collective-permute-start | bytes 196616 | tf_op jit(solution)/shard_map/while/body/eval_jaxpr/ppermute | solution.py:12
  366.2 9.9 %collective-permute-start = (f32[128,128]{1,0:T(8,128)S(1)}, f32[128,128]{1,0:T(8,128)S(1)}, u32[]{:S(2)}, u32[]{:S(2)}) collective-permute-start(f32[128,128]{1,0:T(8,128)S(1)} %get-tuple-element.487), channel_id=1, source_target_pairs={{15,0},{0,1},{1,2},{2,3},{3,4},{4,5},{5,6},{6,7},{7,8},{8,9},{9,10... | collective-permute-start | bytes 196616 | tf_op jit(solution)/shard_map/while/body/eval_jaxpr/ppermute | solution.py:12
  376.1 9.3 %collective-permute-start = (f32[128,128]{1,0:T(8,128)S(1)}, f32[128,128]{1,0:T(8,128)S(1)}, u32[]{:S(2)}, u32[]{:S(2)}) collective-permute-start(f32[128,128]{1,0:T(8,128)S(1)} %get-tuple-element.487), channel_id=1, source_target_pairs={{15,0},{0,1},{1,2},{2,3},{3,4},{4,5},{5,6},{6,7},{7,8},{8,9},{9,10... | collective-permute-start | bytes 196616 | tf_op jit(solution)/shard_map/while/body/eval_jaxpr/ppermute | solution.py:12
  385.4 10.6 %collective-permute-start = (f32[128,128]{1,0:T(8,128)S(1)}, f32[128,128]{1,0:T(8,128)S(1)}, u32[]{:S(2)}, u32[]{:S(2)}) collective-permute-start(f32[128,128]{1,0:T(8,128)S(1)} %get-tuple-element.487), channel_id=1, source_target_pairs={{15,0},{0,1},{1,2},{2,3},{3,4},{4,5},{5,6},{6,7},{7,8},{8,9},{9,10... | collective-permute-start | bytes 196616 | tf_op jit(solution)/shard_map/while/body/eval_jaxpr/ppermute | solution.py:12
  396.0 9.5 %collective-permute-start = (f32[128,128]{1,0:T(8,128)S(1)}, f32[128,128]{1,0:T(8,128)S(1)}, u32[]{:S(2)}, u32[]{:S(2)}) collective-permute-start(f32[128,128]{1,0:T(8,128)S(1)} %get-tuple-element.487), channel_id=1, source_target_pairs={{15,0},{0,1},{1,2},{2,3},{3,4},{4,5},{5,6},{6,7},{7,8},{8,9},{9,10... | collective-permute-start | bytes 196616 | tf_op jit(solution)/shard_map/while/body/eval_jaxpr/ppermute | solution.py:12
  405.5 10.2 %collective-permute-start = (f32[128,128]{1,0:T(8,128)S(1)}, f32[128,128]{1,0:T(8,128)S(1)}, u32[]{:S(2)}, u32[]{:S(2)}) collective-permute-start(f32[128,128]{1,0:T(8,128)S(1)} %get-tuple-element.487), channel_id=1, source_target_pairs={{15,0},{0,1},{1,2},{2,3},{3,4},{4,5},{5,6},{6,7},{7,8},{8,9},{9,10... | collective-permute-start | bytes 196616 | tf_op jit(solution)/shard_map/while/body/eval_jaxpr/ppermute | solution.py:12
  415.8 10.1 %collective-permute-start = (f32[128,128]{1,0:T(8,128)S(1)}, f32[128,128]{1,0:T(8,128)S(1)}, u32[]{:S(2)}, u32[]{:S(2)}) collective-permute-start(f32[128,128]{1,0:T(8,128)S(1)} %get-tuple-element.487), channel_id=1, source_target_pairs={{15,0},{0,1},{1,2},{2,3},{3,4},{4,5},{5,6},{6,7},{7,8},{8,9},{9,10... | collective-permute-start | bytes 196616 | tf_op jit(solution)/shard_map/while/body/eval_jaxpr/ppermute | solution.py:12
  425.9 9.2 %collective-permute-start = (f32[128,128]{1,0:T(8,128)S(1)}, f32[128,128]{1,0:T(8,128)S(1)}, u32[]{:S(2)}, u32[]{:S(2)}) collective-permute-start(f32[128,128]{1,0:T(8,128)S(1)} %get-tuple-element.487), channel_id=1, source_target_pairs={{15,0},{0,1},{1,2},{2,3},{3,4},{4,5},{5,6},{6,7},{7,8},{8,9},{9,10... | collective-permute-start | bytes 196616 | tf_op jit(solution)/shard_map/while/body/eval_jaxpr/ppermute | solution.py:12
  435.2 9.2 %collective-permute-start = (f32[128,128]{1,0:T(8,128)S(1)}, f32[128,128]{1,0:T(8,128)S(1)}, u32[]{:S(2)}, u32[]{:S(2)}) collective-permute-start(f32[128,128]{1,0:T(8,128)S(1)} %get-tuple-element.487), channel_id=1, source_target_pairs={{15,0},{0,1},{1,2},{2,3},{3,4},{4,5},{5,6},{6,7},{7,8},{8,9},{9,10... | collective-permute-start | bytes 196616 | tf_op jit(solution)/shard_map/while/body/eval_jaxpr/ppermute | solution.py:12
  444.4 9.2 %collective-permute-start = (f32[128,128]{1,0:T(8,128)S(1)}, f32[128,128]{1,0:T(8,128)S(1)}, u32[]{:S(2)}, u32[]{:S(2)}) collective-permute-start(f32[128,128]{1,0:T(8,128)S(1)} %get-tuple-element.487), channel_id=1, source_target_pairs={{15,0},{0,1},{1,2},{2,3},{3,4},{4,5},{5,6},{6,7},{7,8},{8,9},{9,10... | collective-permute-start | bytes 196616 | tf_op jit(solution)/shard_map/while/body/eval_jaxpr/ppermute | solution.py:12
Sparse Core Ops, SparseCore 0:
  89.4 120.9 reduce-scatter.1
  213.1 67.2 all-gather.1
  286.0 265.3 all-reduce.1
where the time goes:
time: 561 us; the launch traced here: 560 us
  waiting for transfers between devices  399 us (71%)
  blocking collectives  48.6 us (9%)
  matrix products  39.9 us (7%)
  starting transfers between devices  28.9 us (5%)
  local copies, waits for them, and re-layouts  20.9 us (4%)
  between operations  14.5 us (3%)
  other arithmetic  6.2 us (1%)
    reduce_scatter x1, waiting for transfers between devices, local(): lax.psum_scatter(partial_rows, 'rep', scatter_dimension=0, tiled=True)  121 us
    ppermute x15, waiting for transfers between devices, from_behind(): return lax.ppermute(block, axis, route)  115 us
    psum x1, waiting for transfers between devices, local(): weight_grad = lax.psum(weight_term, ('rep', 'row'))  97.1 us
    all_gather x1, waiting for transfers between devices, local(): grad_rows = lax.all_gather(grad_hidden, 'rep', axis=0, tiled=True)  65.7 us
    all_gather x1, blocking collectives, local(): lax.all_gather(features, 'row', axis=0, tiled=True)  48.6 us
    ppermute x15, starting transfers between devices, from_behind(): return lax.ppermute(block, axis, route)  28.8 us
    dot_general x8, matrix products, advance(): jnp.einsum('rt,tif->rif', select, product, precision=lax.Precision.HIGHEST)  21.6 us
    gather x8, local copies, waits for them, and re-layouts, advance(): picked = jnp.take(sources, coord_block[:, pick_column], axis=0)  15 us
  transfers between devices with their start and end apart: 18, of which 18 were waited for; matrix products, arithmetic and copies ran while one was open for 5% of the time, Pallas kernels for 0%

commit v1 on v0

--- a/solution.py
+++ b/solution.py
@@ -4,12 +4,6 @@
 import jax.numpy as jnp
 from jax import lax
 from jax.sharding import PartitionSpec as P
-
-
-def from_behind(block, axis, distance):
-    devices = range(lax.axis_size(axis))
-    route = [((i - distance) % len(devices), i) for i in devices]
-    return lax.ppermute(block, axis, route)
 
 
 def silu_slope(preactivation):
@@ -49,42 +43,44 @@
     row_count = lax.axis_size("row")
     tile_size = features.shape[0]
     feature_size = features.shape[1]
+    hidden_size = weight.shape[1]
     values = tile_values[0, 0]
     coords = tile_coords[0, 0]
     live_count = tile_count[0, 0]
-    columns = lax.all_gather(features, "row", axis=0, tiled=True).reshape(
-        row_count, tile_size, feature_size
+    columns = lax.all_to_all(
+        jnp.broadcast_to(features[None], (row_count, tile_size, feature_size)), "row", 0, 0, tiled=True
     )
     partial_rows = tile_products(values, coords, live_count, columns, rep_count, False)
-    partial_rows = partial_rows.reshape(rep_count * tile_size, feature_size)
-    aggregated = lax.psum_scatter(partial_rows, "rep", scatter_dimension=0, tiled=True).astype(
-        jnp.bfloat16
-    )
+    received = lax.all_to_all(partial_rows, "rep", 0, 0, tiled=True)
+    aggregated = jnp.sum(received, axis=0).astype(jnp.bfloat16)
     preactivation = jnp.dot(aggregated, weight, preferred_element_type=jnp.float32)
     grad_pre = (cotangent.astype(jnp.float32) * silu_slope(preactivation)).astype(jnp.bfloat16)
     grad_hidden = lax.dot_general(
         grad_pre, weight, (((1,), (1,)), ((), ())), preferred_element_type=jnp.float32
     ).astype(jnp.bfloat16)
-    grad_rows = lax.all_gather(grad_hidden, "rep", axis=0, tiled=True)
+    grad_blocks = lax.all_to_all(
+        jnp.broadcast_to(grad_hidden[None], (rep_count, tile_size, feature_size)), "rep", 0, 0, tiled=True
+    )
     activated = jax.nn.silu(preactivation).astype(jnp.bfloat16)
-    grad_blocks = grad_rows.reshape(rep_count, tile_size, feature_size)
     back_terms = tile_products(values, coords, live_count, grad_blocks, row_count, True)
-    row_place = lax.axis_index("row")
-
-    def pass_on(turn_index, carried):
-        carried = from_behind(carried, "row", 1)
-        target = (row_place + row_count - 1 - turn_index) % row_count
-        return carried + lax.dynamic_index_in_dim(back_terms, target, 0, keepdims=False)
-
-    initial = lax.dynamic_index_in_dim(
-        back_terms, (row_place + row_count - 1) % row_count, 0, keepdims=False
-    )
-    feature_sum = lax.fori_loop(1, row_count, pass_on, initial)
-    feature_grad = feature_sum.astype(jnp.bfloat16)
     weight_term = lax.dot_general(
         aggregated, grad_pre, (((0,), (0,)), ((), ())), preferred_element_type=jnp.float32
     )
-    weight_grad = lax.psum(weight_term, ("rep", "row"))
+    chunk_rows = feature_size * hidden_size // (row_count * feature_size)
+    weight_chunks = weight_term.reshape(row_count, chunk_rows, feature_size)
+    outgoing = jnp.concatenate([back_terms, weight_chunks], axis=1)
+    incoming = jnp.sum(lax.all_to_all(outgoing, "row", 0, 0, tiled=True), axis=0)
+    feature_grad = incoming[:tile_size].astype(jnp.bfloat16)
+    row_chunk = incoming[tile_size:]
+    rep_summed = jnp.sum(
+        lax.all_to_all(
+            jnp.broadcast_to(row_chunk[None], (rep_count,) + row_chunk.shape), "rep", 0, 0, tiled=True
+        ),
+        axis=0,
+    )
+    weight_grad = lax.all_to_all(
+        jnp.broadcast_to(rep_summed[None], (row_count,) + rep_summed.shape), "row", 0, 0, tiled=True
+    ).reshape(feature_size, hidden_size)
     return (activated, feature_grad, weight_grad)
 
 

time: 561 us -> 251 us (0.45)
  waiting for transfers between devices: 399 us -> 42.4 us
  blocking collectives: 48.6 us -> 129 us
  between operations: 14.5 us -> 1.44 us
  matrix products: 39.9 us -> 27.8 us
  starting transfers between devices: 28.9 us -> 21.5 us
    all_to_all x0 -> x3, blocking collectives: none -> 129 us  [the longest x1 71.6 us: local(): received = lax.all_to_all(partial_rows, 'rep', 0, 0, tiled=True)]
    reduce_scatter x1 -> x0, waiting for transfers between devices: 121 us -> none  [local(): lax.psum_scatter(partial_rows, 'rep', scatter_dimension=0, tiled=True)]
    ppermute x15 -> x0, waiting for transfers between devices: 115 us -> none  [from_behind(): return lax.ppermute(block, axis, route)]
    psum x1 -> x0, waiting for transfers between devices: 97.1 us -> none  [local(): weight_grad = lax.psum(weight_term, ('rep', 'row'))]
    all_gather x1 -> x0, waiting for transfers between devices: 65.7 us -> none  [local(): grad_rows = lax.all_gather(grad_hidden, 'rep', axis=0, tiled=True)]
    all_gather x1 -> x0, blocking collectives: 48.6 us -> none  [local(): lax.all_gather(features, 'row', axis=0, tiled=True)]
    all_to_all x0 -> x3, waiting for transfers between devices: none -> 42.4 us  [the longest x1 21.4 us: local(): lax.all_to_all(jnp.broadcast_to(grad_hidden[None], (rep_count, tile_size,...]
    ppermute x15 -> x0, starting transfers between devices: 28.8 us -> none  [from_behind(): return lax.ppermute(block, axis, route)]
  transfers between devices with their start and end apart: 18 -> 3, of which waited for: 18 -> 3; matrix products, arithmetic and copies ran while one was open for 5% -> 3% of each run, Pallas kernels for 0% -> 0%
where the time goes in v1:
time: 251 us; the launch traced here: 249 us
  blocking collectives  129 us (51%)
  waiting for transfers between devices  42.4 us (17%)
  matrix products  27.8 us (11%)
  local copies, waits for them, and re-layouts  22.8 us (9%)
  starting transfers between devices  21.5 us (9%)
  other arithmetic  4.36 us (2%)
    all_to_all x1, blocking collectives, local(): received = lax.all_to_all(partial_rows, 'rep', 0, 0, tiled=True)  71.6 us
    all_to_all x1, blocking collectives, local(): lax.all_to_all(outgoing, 'row', 0, 0, tiled=True)  35.5 us
    all_to_all x1, blocking collectives, local(): lax.all_to_all(jnp.broadcast_to(row_chunk[None], (rep_count,) + row_chunk...  21.7 us
    all_to_all x1, waiting for transfers between devices, local(): lax.all_to_all(jnp.broadcast_to(grad_hidden[None], (rep_count, tile_size,...  21.4 us
    dot_general x6, matrix products, advance(): jnp.einsum('rt,tif->rif', select, product, precision=lax.Precision.HIGHEST)  16.2 us
    all_to_all x1, starting transfers between devices, local(): lax.all_to_all(jnp.broadcast_to(features[None], (row_count, tile_size, fe...  13.4 us
    all_to_all x1, waiting for transfers between devices, local(): lax.all_to_all(jnp.broadcast_to(features[None], (row_count, tile_size, fe...  12.3 us
    dot_general x6, matrix products, advance(): jnp.einsum(form, tile_block, picked, preferred_element_type=jnp.float32)  10.4 us
  transfers between devices with their start and end apart: 3, of which 3 were waited for; matrix products, arithmetic and copies ran while one was open for 3% of the time, Pallas kernels for 0%

profile of v1, /device:TPU:1, one launch (start us, length us, event | category | flops | bytes accessed | tf_op | source)
XLA Modules:
  0.0 249.5 jit_solution(9770018288099859573)
XLA Ops:
  0.7 1.7 broadcast_in_dim.37
  2.3 13.4 %all-to-all-start = ((bf16[16,128,128]{2,1,0:T(8,128)(2,1)}), bf16[16,128,128]{2,1,0:T(8,128)(2,1)S(1)}, u32[]{:S(2)}, u32[]{:S(2)}) async-start(bf16[16,128,128]{2,1,0:T(8,128)(2,1)} %broadcast_in_dim.37), calls=%async_computation | async-start | bytes 1048576 | tf_op jit(solution)/shard_map/all_to_all | solution.py:50
  16.4 12.3 %all-to-all-done = bf16[16,128,128]{2,1,0:T(8,128)(2,1)S(1)} async-done(((bf16[16,128,128]{2,1,0:T(8,128)(2,1)}), bf16[16,128,128]{2,1,0:T(8,128)(2,1)S(1)}, u32[]{:S(2)}, u32[]{:S(2)}) %all-to-all-start) | async-done | bytes 524320 | tf_op jit(solution)/shard_map/all_to_all | solution.py:50
  28.7 0.8 copy-done.1
  29.5 0.2 broadcast_in_dim.36
  29.8 22.4 %while.22 = (s32[]{:T(128)}, f32[32,128,128]{2,0,1:T(8,128)S(1)}, s32[]{:T(128)}, s32[128,2]{0,1:T(2,128)S(1)}, s32[]{:T(128)}, /*index=5*/bf16[128,128,128]{2,1...) while((s32[]{:T(128)}, f32[32,128,128]{2,0,1:T(8,128)S(1)}, ...), condition=%wide.region_1.2_spmd.clone, body=%wide.region_0.1_spmd.clone.sunk | while | flops 336596320 | bytes 12588843 | solution.py:38
  29.9 1.8 gather_fusion
  31.7 1.7 fusion.67
  33.5 0.7 add_compare_fusion.4
  34.1 3.1 %fusion.68 = f32[32,128,128]{2,0,1:T(8,128)S(1)} fusion(f32[32,128,128]{2,0,1:T(8,128)S(1)} %get-tuple-element.274, f32[32,128,128]{2,1,0:T(8,128)S(1)} %fusion.67, s32[32]{0:T(128)S(1)} %get-tuple-element.252, pred[32]{0:T(512)(128)(4,1)S(1)} %add_compare_fusion.4), kind=kOutput, calls=%fused_computation.6.clone.1 | convolution fusion | flops 201852928 | bytes 6291616 | tf_op jit(solution)/shard_map/while/body/rt,tif->rif/dot_general | solution.py:35
  37.4 1.8 gather_fusion
  39.2 1.7 fusion.67
  40.9 0.7 add_compare_fusion.4
  41.6 3.1 %fusion.68 = f32[32,128,128]{2,0,1:T(8,128)S(1)} fusion(f32[32,128,128]{2,0,1:T(8,128)S(1)} %get-tuple-element.274, f32[32,128,128]{2,1,0:T(8,128)S(1)} %fusion.67, s32[32]{0:T(128)S(1)} %get-tuple-element.252, pred[32]{0:T(512)(128)(4,1)S(1)} %add_compare_fusion.4), kind=kOutput, calls=%fused_computation.6.clone.1 | convolution fusion | flops 201852928 | bytes 6291616 | tf_op jit(solution)/shard_map/while/body/rt,tif->rif/dot_general | solution.py:35
  44.9 1.8 gather_fusion
  46.7 1.7 fusion.67
  48.4 0.7 add_compare_fusion.4
  49.1 3.1 %fusion.68 = f32[32,128,128]{2,0,1:T(8,128)S(1)} fusion(f32[32,128,128]{2,0,1:T(8,128)S(1)} %get-tuple-element.274, f32[32,128,128]{2,1,0:T(8,128)S(1)} %fusion.67, s32[32]{0:T(128)S(1)} %get-tuple-element.252, pred[32]{0:T(512)(128)(4,1)S(1)} %add_compare_fusion.4), kind=kOutput, calls=%fused_computation.6.clone.1 | convolution fusion | flops 201852928 | bytes 6291616 | tf_op jit(solution)/shard_map/while/body/rt,tif->rif/dot_general | solution.py:35
  52.2 1.2 copy.16
  53.5 71.6 %all_to_all.30 = f32[32,128,128]{2,1,0:T(8,128)S(1)} all-to-all(f32[32,128,128]{2,1,0:T(8,128)S(1)} %copy.16), channel_id=1, replica_groups=mesh['rep'=32,'row'=16] {'rep'}, dimensions={0} | all-to-all | bytes 4194304 | tf_op jit(solution)/shard_map/all_to_all | solution.py:54
  125.1 0.7 copy-done.3
  125.8 0.8 multiply_convert_fusion
  126.8 1.2 broadcast_in_dim.57
  128.1 4.3 %all-to-all-start.2 = ((bf16[32,128,128]{2,1,0:T(8,128)(2,1)}), bf16[32,128,128]{2,1,0:T(8,128)(2,1)S(1)}, u32[]{:S(2)}, u32[]{:S(2)}) async-start(bf16[32,128,128]{2,1,0:T(8,128)(2,1)} %broadcast_in_dim.57), calls=%async_computation.2 | async-start | bytes 2097152 | tf_op jit(solution)/shard_map/all_to_all | solution.py:61
  132.4 6.4 %copy.14 = bf16[1,1,128,128,128]{3,4,2,1,0:T(8,128)(2,1)} copy(bf16[1,1,128,128,128]{4,3,2,1,0:T(8,128)(2,1)} %bitcast.42) | data formatting | bytes 8388608 | tf_op args[3]
  138.8 0.2 fusion.44
  139.0 21.4 %all-to-all-done.2 = bf16[32,128,128]{2,1,0:T(8,128)(2,1)S(1)} async-done(((bf16[32,128,128]{2,1,0:T(8,128)(2,1)}), bf16[32,128,128]{2,1,0:T(8,128)(2,1)S(1)}, u32[]{:S(2)}, u32[]{:S(2)}) %all-to-all-start.2) | async-done | bytes 1048608 | tf_op jit(solution)/shard_map/all_to_all | solution.py:61
  160.5 16.7 %while.23 = (s32[]{:T(128)}, f32[16,128,128]{2,0,1:T(8,128)S(1)}, s32[]{:T(128)}, s32[128,2]{0,1:T(2,128)S(1)}, s32[]{:T(128)}, /*index=5*/bf16[128,128,128]{1,2...) while((s32[]{:T(128)}, f32[16,128,128]{2,0,1:T(8,128)S(1)}, ...), condition=%wide.region_4.5_spmd.clone, body=%wide.region_3.4_spmd.clone.sunk | while | flops 235669856 | bytes 10491691 | solution.py:38
  160.6 0.7 gather_fusion.1
  161.4 1.7 fusion.73
  163.1 0.7 add_compare_fusion.5
  163.8 2.3 fusion.74
  166.2 0.7 gather_fusion.1
  166.9 1.7 fusion.73
  168.7 0.7 add_compare_fusion.5
  169.3 2.3 fusion.74
  171.7 0.7 gather_fusion.1
  172.5 1.7 fusion.73
  174.2 0.7 add_compare_fusion.5
  174.9 2.3 fusion.74
  177.2 0.3 copy.17
  177.6 35.5 %all_to_all.31 = f32[16,144,128]{2,1,0:T(8,128)S(1)} all-to-all(f32[16,144,128]{2,1,0:T(8,128)S(1)} %pad_maximum_fusion), channel_id=1, replica_groups=mesh['rep'=32,'row'=16] {'row'}, dimensions={0} | all-to-all | bytes 2359296 | tf_op jit(solution)/shard_map/all_to_all | solution.py:72
  213.2 21.7 %all_to_all.32 = f32[32,16,128]{2,1,0:T(8,128)S(1)} all-to-all(f32[32,16,128]{2,1,0:T(8,128)S(1)} %broadcast_in_dim.58), channel_id=1, replica_groups=mesh['rep'=32,'row'=16] {'rep'}, dimensions={0} | all-to-all | bytes 524288 | tf_op jit(solution)/shard_map/all_to_all | solution.py:76
  235.0 0.7 broadcast_in_dim.59
  235.6 3.8 %all-to-all-start.5 = ((f32[16,16,128]{2,1,0:T(8,128)}), f32[16,16,128]{2,1,0:T(8,128)S(1)}, u32[]{:S(2)}, u32[]{:S(2)}) async-start(f32[16,16,128]{2,1,0:T(8,128)} %broadcast_in_dim.59), calls=%async_computation.5 | async-start | bytes 262144 | tf_op jit(solution)/shard_map/all_to_all | solution.py:81
  239.4 0.6 slice.44
  240.1 8.7 %all-to-all-done.5 = f32[16,16,128]{2,1,0:T(8,128)S(1)} async-done(((f32[16,16,128]{2,1,0:T(8,128)}), f32[16,16,128]{2,1,0:T(8,128)S(1)}, u32[]{:S(2)}, u32[]{:S(2)}) %all-to-all-start.5) | async-done | bytes 131104 | tf_op jit(solution)/shard_map/all_to_all | solution.py:81
  248.8 0.7 reshape.39
  (39 shorter events, 1.2 us)
Async XLA Ops:
  0.6 124.5 %copy-start = (bf16[128,256]{1,0:T(8,128)(2,1)S(1)}, bf16[128,256]{1,0:T(8,128)(2,1)}, u32[]{:S(2)}) copy-start(bf16[128,256]{1,0:T(8,128)(2,1)} %param.11) | copy-start | bytes 196612
  0.6 29.1 %copy-start.2 = (s32[1,1,128,2]{2,3,1,0:T(2,128)S(1)}, s32[1,1,128,2]{2,3,1,0:T(2,128)}, u32[]{:S(2)}) copy-start(s32[1,1,128,2]{2,3,1,0:T(2,128)} %param.14) | copy-start | bytes 3076
  2.3 26.4 %all-to-all-start = ((bf16[16,128,128]{2,1,0:T(8,128)(2,1)}), bf16[16,128,128]{2,1,0:T(8,128)(2,1)S(1)}, u32[]{:S(2)}, u32[]{:S(2)}) async-start(bf16[16,128,128]{2,1,0:T(8,128)(2,1)} %broadcast_in_dim.37), calls=%async_computation | async-start | bytes 1048576 | tf_op jit(solution)/shard_map/all_to_all | solution.py:50
  28.7 0.8 copy-start.1
  125.0 0.8 copy-start.3
  128.1 32.4 %all-to-all-start.2 = ((bf16[32,128,128]{2,1,0:T(8,128)(2,1)}), bf16[32,128,128]{2,1,0:T(8,128)(2,1)S(1)}, u32[]{:S(2)}, u32[]{:S(2)}) async-start(bf16[32,128,128]{2,1,0:T(8,128)(2,1)} %broadcast_in_dim.57), calls=%async_computation.2 | async-start | bytes 2097152 | tf_op jit(solution)/shard_map/all_to_all | solution.py:61
  235.6 13.1 %all-to-all-start.5 = ((f32[16,16,128]{2,1,0:T(8,128)}), f32[16,16,128]{2,1,0:T(8,128)S(1)}, u32[]{:S(2)}, u32[]{:S(2)}) async-start(f32[16,16,128]{2,1,0:T(8,128)} %broadcast_in_dim.59), calls=%async_computation.5 | async-start | bytes 262144 | tf_op jit(solution)/shard_map/all_to_all | solution.py:81

commit v2 on v1

--- a/solution.py
+++ b/solution.py
@@ -3,7 +3,12 @@
 import jax
 import jax.numpy as jnp
 from jax import lax
+from jax.experimental import pallas as pl
+from jax.experimental.pallas import tpu as pltpu
 from jax.sharding import PartitionSpec as P
+
+
+SLOTS_STEP = 16
 
 
 def silu_slope(preactivation):
@@ -12,30 +17,61 @@
 
 
 def tile_products(values, coords, live_count, sources, buckets, adjoint):
-    slot_total = values.shape[0]
-    tile_size = values.shape[1]
-    width = sources.shape[2]
-    group_size = math.gcd(slot_total, 32)
-    round_total = (live_count + group_size - 1) // group_size
-    bucket_ids = jnp.arange(buckets, dtype=jnp.int32)
-    pick_column = 0 if adjoint else 1
-    sum_column = 1 if adjoint else 0
-    form = "tji,tjf->tif" if adjoint else "tij,tjf->tif"
+    slot_total, tile_size, _ = values.shape
+    source_total, _, width = sources.shape
+    step = math.gcd(slot_total, SLOTS_STEP)
+    pick = 0 if adjoint else 1
+    put = 1 if adjoint else 0
+    flat_coords = coords.reshape(-1).astype(jnp.int32)
+    live = jnp.reshape(live_count, (1,)).astype(jnp.int32)
 
-    def advance(turn_index, running):
-        begin_at = turn_index * group_size
-        tile_block = lax.dynamic_slice_in_dim(values, begin_at, group_size, 0)
-        coord_block = lax.dynamic_slice_in_dim(coords, begin_at, group_size, 0)
-        live_mask = begin_at + jnp.arange(group_size, dtype=jnp.int32) < live_count
-        picked = jnp.take(sources, coord_block[:, pick_column], axis=0)
-        product = jnp.einsum(form, tile_block, picked, preferred_element_type=jnp.float32)
-        select = (
-            (coord_block[:, sum_column][None, :] == bucket_ids[:, None]) & live_mask[None, :]
-        ).astype(jnp.float32)
-        return running + jnp.einsum("rt,tif->rif", select, product, precision=lax.Precision.HIGHEST)
+    def kernel(coord_ref, live_ref, value_ref, source_ref, out_ref):
+        first = pl.program_id(0) * step
 
-    start_sum = jnp.zeros((buckets, tile_size, width), jnp.float32)
-    return lax.fori_loop(0, round_total, advance, start_sum)
+        @pl.when(pl.program_id(0) == 0)
+        def _():
+            out_ref[...] = jnp.zeros_like(out_ref)
+
+        def one(k, carry):
+            slot = first + k
+
+            @pl.when(slot < live_ref[0])
+            def _():
+                source_at = jnp.clip(coord_ref[2 * slot + pick], 0, source_total - 1)
+                put_at = jnp.clip(coord_ref[2 * slot + put], 0, buckets - 1)
+                tile = value_ref[k]
+                source = source_ref[source_at]
+                if adjoint:
+                    product = lax.dot_general(
+                        tile, source, (((0,), (0,)), ((), ())), preferred_element_type=jnp.float32
+                    )
+                else:
+                    product = jnp.dot(tile, source, preferred_element_type=jnp.float32)
+                out_ref[put_at] += product
+
+            return carry
+
+        lax.fori_loop(0, step, one, 0, unroll=True)
+
+    def value_index(i, coord_ref, live_ref):
+        last = jnp.maximum(live_ref[0] - 1, 0) // step
+        return (jnp.minimum(i, last), 0, 0)
+
+    grid_spec = pltpu.PrefetchScalarGridSpec(
+        num_scalar_prefetch=2,
+        grid=(slot_total // step,),
+        in_specs=[
+            pl.BlockSpec((step, tile_size, tile_size), value_index),
+            pl.BlockSpec((source_total, tile_size, width), lambda i, c, l: (0, 0, 0)),
+        ],
+        out_specs=pl.BlockSpec((buckets, tile_size, width), lambda i, c, l: (0, 0, 0)),
+    )
+    return pl.pallas_call(
+        kernel,
+        grid_spec=grid_spec,
+        out_shape=jax.ShapeDtypeStruct((buckets, tile_size, width), jnp.float32),
+        compiler_params=pltpu.CompilerParams(dimension_semantics=("arbitrary",)),
+    )(flat_coords, live, values, sources)
 
 
 def local(features, weight, cotangent, tile_values, tile_coords, tile_count):

time: 251 us -> 245 us (0.976)
  Pallas kernels: 0 us -> 28.4 us
  matrix products: 27.8 us -> 1.17 us
  local copies, waits for them, and re-layouts: 22.8 us -> 8.23 us
  waiting for transfers between devices: 42.4 us -> 48 us
  blocking collectives: 129 us -> 134 us
  other arithmetic: 4.36 us -> 1.51 us
    pallas_call x0 -> x2, Pallas kernels: none -> 28.4 us  [tile_products(): pl.pallas_call(kernel, grid_spec=grid_spec, out_shape=jax.ShapeDtypeStruc...]
    dot_general x12 -> x0, matrix products: 26.6 us -> none  [the longest x6 16.2 us: advance(): jnp.einsum('rt,tif->rif', select, product, precision=lax.Precision.HIGHEST)]
    gather x6 -> x0, local copies, waits for them, and re-layouts: 7.61 us -> none  [advance(): picked = jnp.take(sources, coord_block[:, pick_column], axis=0)]
    all_to_all x1, waiting for transfers between devices: 21.4 us -> 27.8 us  [local(): lax.all_to_all(jnp.broadcast_to(grad_hidden[None], (rep_count, tile_size,...]
    unnamed x9 -> x11, local copies, waits for them, and re-layouts: 7.9 us -> 2.61 us
    lt x6 -> x0, other arithmetic: 3.92 us -> none  [advance(): live_mask = begin_at + jnp.arange(group_size, dtype=jnp.int32) < live_count]
    all_to_all x1, blocking collectives: 21.7 us -> 25 us  [local(): lax.all_to_all(jnp.broadcast_to(row_chunk[None], (rep_count,) + row_chunk...]
  transfers between devices with their start and end apart: 3 -> 3, of which waited for: 3 -> 3; matrix products, arithmetic and copies ran while one was open for 3% -> 1% of each run, Pallas kernels for 0% -> 0%
where the time goes in v2:
time: 245 us; the launch traced here: 244 us
  blocking collectives  134 us (55%)
  waiting for transfers between devices  48 us (20%)
  Pallas kernels  28.4 us (12%)
  starting transfers between devices  21.5 us (9%)
  local copies, waits for them, and re-layouts  8.23 us (3%)
    all_to_all x1, blocking collectives, local(): received = lax.all_to_all(partial_rows, 'rep', 0, 0, tiled=True)  71.8 us
    all_to_all x1, blocking collectives, local(): lax.all_to_all(outgoing, 'row', 0, 0, tiled=True)  36.8 us
    pallas_call x2, Pallas kernels, tile_products(): pl.pallas_call(kernel, grid_spec=grid_spec, out_shape=jax.ShapeDtypeStruc...  28.4 us
    all_to_all x1, waiting for transfers between devices, local(): lax.all_to_all(jnp.broadcast_to(grad_hidden[None], (rep_count, tile_size,...  27.8 us
    all_to_all x1, blocking collectives, local(): lax.all_to_all(jnp.broadcast_to(row_chunk[None], (rep_count,) + row_chunk...  25 us
    all_to_all x1, starting transfers between devices, local(): lax.all_to_all(jnp.broadcast_to(features[None], (row_count, tile_size, fe...  13.4 us
    all_to_all x1, waiting for transfers between devices, local(): lax.all_to_all(jnp.broadcast_to(features[None], (row_count, tile_size, fe...  11.5 us
    all_to_all x1, waiting for transfers between devices, local(): lax.all_to_all(jnp.broadcast_to(rep_summed[None], (row_count,) + rep_summ...  8.69 us
  transfers between devices with their start and end apart: 3, of which 3 were waited for; matrix products, arithmetic and copies ran while one was open for 1% of the time, Pallas kernels for 0%

profile of v2, /device:TPU:1, one launch (start us, length us, event | category | flops | bytes accessed | tf_op | source)
XLA Modules:
  0.0 243.7 jit_solution(10365284175641125971)
XLA Ops:
  0.6 0.0 copy-start
  0.6 0.0 copy-start.3
  0.7 1.7 broadcast_in_dim.8
  2.3 13.4 %all-to-all-start = ((bf16[16,128,128]{2,1,0:T(8,128)(2,1)}), bf16[16,128,128]{2,1,0:T(8,128)(2,1)S(1)}, u32[]{:S(2)}, u32[]{:S(2)}) async-start(bf16[16,128,128]{2,1,0:T(8,128)(2,1)} %broadcast_in_dim.8), calls=%async_computation | async-start | bytes 1048576 | tf_op jit(solution)/shard_map/all_to_all | solution.py:86
  16.4 0.0 copy-done.3
  16.4 0.1 copy.10
  16.5 0.7 reshape_squeeze.8.coord_ref
  17.2 11.5 %all-to-all-done.source_ref = bf16[16,128,128]{2,1,0:T(8,128)(2,1)S(1)} async-done(((bf16[16,128,128]{2,1,0:T(8,128)(2,1)}), bf16[16,128,128]{2,1,0:T(8,128)(2,1)S(1)}, u32[]{:S(2)}, u32[]{:S(2)}) %all-to-all-start) | async-done | bytes 524320 | tf_op jit(solution)/shard_map/all_to_all | solution.py:86
  28.7 0.0 copy-start.2
  28.7 0.8 copy-done.2
  29.5 12.8 %shard_map.85 = f32[32,128,128]{2,1,0:T(8,128)} custom-call(s32[256]{0:T(256)} %reshape_squeeze.8.coord_ref, s32[1]{0:T(128)} %bitcast.10.live_ref, bf16[128,128,128]{2,1,0:T(8,128)(2,1)} %bitcast.12, bf16[16,128,128]{2,1,0:T(8,128)(2,1)} %copy-done.2), custom_call_target="tpu_custom_call" | custom-call | tf_op jit(solution)/shard_map/pallas_call | solution.py:69
  42.3 71.8 %all_to_all.30 = f32[32,128,128]{2,1,0:T(8,128)S(1)} all-to-all(f32[32,128,128]{2,1,0:T(8,128)} %shard_map.85), channel_id=1, replica_groups=mesh['rep'=32,'row'=16] {'rep'}, dimensions={0} | all-to-all | bytes 4194304 | tf_op jit(solution)/shard_map/all_to_all | solution.py:90
  114.1 0.0 copy-start.4
  114.1 0.1 reduce_sum.27
  114.2 0.0 copy-done
  114.2 0.7 copy-done.4
  114.9 0.8 multiply_convert_fusion
  115.8 0.2 convolution_convert_fusion
  115.9 1.2 broadcast_in_dim.9
  117.1 4.3 %all-to-all-start.2 = ((bf16[32,128,128]{2,1,0:T(8,128)(2,1)}), bf16[32,128,128]{2,1,0:T(8,128)(2,1)S(1)}, u32[]{:S(2)}, u32[]{:S(2)}) async-start(bf16[32,128,128]{2,1,0:T(8,128)(2,1)} %broadcast_in_dim.9), calls=%async_computation.2 | async-start | bytes 2097152 | tf_op jit(solution)/shard_map/all_to_all | solution.py:97
  121.5 0.2 fusion.4
  121.7 27.8 %all-to-all-done.2.source_ref = bf16[32,128,128]{2,1,0:T(8,128)(2,1)S(1)} async-done(((bf16[32,128,128]{2,1,0:T(8,128)(2,1)}), bf16[32,128,128]{2,1,0:T(8,128)(2,1)S(1)}, u32[]{:S(2)}, u32[]{:S(2)}) %all-to-all-start.2) | async-done | bytes 1048608 | tf_op jit(solution)/shard_map/all_to_all | solution.py:97
  149.5 0.0 copy-start.1
  149.5 1.0 copy-done.1
  150.4 15.6 %shard_map.86 = f32[16,128,128]{2,1,0:T(8,128)} custom-call(s32[256]{0:T(256)} %reshape_squeeze.8.coord_ref, s32[1]{0:T(128)} %bitcast.11.live_ref, bf16[128,128,128]{2,1,0:T(8,128)(2,1)} %bitcast.13, bf16[32,128,128]{2,1,0:T(8,128)(2,1)} %copy-done.1), custom_call_target="tpu_custom_call" | custom-call | tf_op jit(solution)/shard_map/pallas_call | solution.py:69
  166.0 1.3 pad_maximum_fusion
  167.3 36.8 %all_to_all.31 = f32[16,144,128]{2,1,0:T(8,128)S(1)} all-to-all(f32[16,144,128]{2,1,0:T(8,128)S(1)} %pad_maximum_fusion), channel_id=1, replica_groups=mesh['rep'=32,'row'=16] {'row'}, dimensions={0} | all-to-all | bytes 2359296 | tf_op jit(solution)/shard_map/all_to_all | solution.py:108
  204.2 0.1 reduce_sum.28
  204.3 25.0 %all_to_all.32 = f32[32,16,128]{2,1,0:T(8,128)S(1)} all-to-all(f32[32,16,128]{2,1,0:T(8,128)S(1)} %broadcast_in_dim.10), channel_id=1, replica_groups=mesh['rep'=32,'row'=16] {'rep'}, dimensions={0} | all-to-all | bytes 524288 | tf_op jit(solution)/shard_map/all_to_all | solution.py:112
  229.3 0.7 broadcast_in_dim.11
  229.9 3.7 %all-to-all-start.5 = ((f32[16,16,128]{2,1,0:T(8,128)}), f32[16,16,128]{2,1,0:T(8,128)S(1)}, u32[]{:S(2)}, u32[]{:S(2)}) async-start(f32[16,16,128]{2,1,0:T(8,128)} %broadcast_in_dim.11), calls=%async_computation.5 | async-start | bytes 262144 | tf_op jit(solution)/shard_map/all_to_all | solution.py:117
  233.7 0.6 slice.12
  234.3 8.7 %all-to-all-done.5 = f32[16,16,128]{2,1,0:T(8,128)S(1)} async-done(((f32[16,16,128]{2,1,0:T(8,128)}), f32[16,16,128]{2,1,0:T(8,128)S(1)}, u32[]{:S(2)}, u32[]{:S(2)}) %all-to-all-start.5) | async-done | bytes 131104 | tf_op jit(solution)/shard_map/all_to_all | solution.py:117
  243.0 0.7 reshape.17
  (4 shorter events, 0.1 us)
Async XLA Ops:
  0.6 113.6 %copy-start = (bf16[128,256]{1,0:T(8,128)(2,1)S(1)}, bf16[128,256]{1,0:T(8,128)(2,1)}, u32[]{:S(2)}) copy-start(bf16[128,256]{1,0:T(8,128)(2,1)} %param.7) | copy-start | bytes 196612
  0.6 15.8 %copy-start.3 = (s32[1,1,128,2]{2,3,1,0:T(2,128)S(1)}, s32[1,1,128,2]{2,3,1,0:T(2,128)}, u32[]{:S(2)}) copy-start(s32[1,1,128,2]{2,3,1,0:T(2,128)} %param.10) | copy-start | bytes 3076
  2.3 26.4 %all-to-all-start = ((bf16[16,128,128]{2,1,0:T(8,128)(2,1)}), bf16[16,128,128]{2,1,0:T(8,128)(2,1)S(1)}, u32[]{:S(2)}, u32[]{:S(2)}) async-start(bf16[16,128,128]{2,1,0:T(8,128)(2,1)} %broadcast_in_dim.8), calls=%async_computation | async-start | bytes 1048576 | tf_op jit(solution)/shard_map/all_to_all | solution.py:86
  28.7 0.8 copy-start.2
  114.1 0.8 copy-start.4
  117.1 32.4 %all-to-all-start.2 = ((bf16[32,128,128]{2,1,0:T(8,128)(2,1)}), bf16[32,128,128]{2,1,0:T(8,128)(2,1)S(1)}, u32[]{:S(2)}, u32[]{:S(2)}) async-start(bf16[32,128,128]{2,1,0:T(8,128)(2,1)} %broadcast_in_dim.9), calls=%async_computation.2 | async-start | bytes 2097152 | tf_op jit(solution)/shard_map/all_to_all | solution.py:97
  149.5 1.0 copy-start.1
  229.9 13.1 %all-to-all-start.5 = ((f32[16,16,128]{2,1,0:T(8,128)}), f32[16,16,128]{2,1,0:T(8,128)S(1)}, u32[]{:S(2)}, u32[]{:S(2)}) async-start(f32[16,16,128]{2,1,0:T(8,128)} %broadcast_in_dim.11), calls=%async_computation.5 | async-start | bytes 262144 | tf_op jit(solution)/shard_map/all_to_all | solution.py:117

commit v3 on v2

--- a/solution.py
+++ b/solution.py
@@ -8,7 +8,7 @@
 from jax.sharding import PartitionSpec as P
 
 
-SLOTS_STEP = 16
+SLOTS_STEP = 32
 
 
 def silu_slope(preactivation):
@@ -32,13 +32,11 @@
         def _():
             out_ref[...] = jnp.zeros_like(out_ref)
 
-        def one(k, carry):
-            slot = first + k
-
-            @pl.when(slot < live_ref[0])
-            def _():
-                source_at = jnp.clip(coord_ref[2 * slot + pick], 0, source_total - 1)
-                put_at = jnp.clip(coord_ref[2 * slot + put], 0, buckets - 1)
+        @pl.when(first < live_ref[0])
+        def _():
+            products = []
+            for k in range(step):
+                source_at = jnp.clip(coord_ref[2 * (first + k) + pick], 0, source_total - 1)
                 tile = value_ref[k]
                 source = source_ref[source_at]
                 if adjoint:
@@ -47,11 +45,12 @@
                     )
                 else:
                     product = jnp.dot(tile, source, preferred_element_type=jnp.float32)
-                out_ref[put_at] += product
-
-            return carry
-
-        lax.fori_loop(0, step, one, 0, unroll=True)
+                products.append(product)
+            for k in range(step):
+                slot = first + k
+                put_at = jnp.clip(coord_ref[2 * slot + put], 0, buckets - 1)
+                kept = jnp.where(slot < live_ref[0], products[k], 0.0)
+                out_ref[put_at] += kept
 
     def value_index(i, coord_ref, live_ref):
         last = jnp.maximum(live_ref[0] - 1, 0) // step

time: 245 us -> 211 us (0.86)
  blocking collectives: 134 us -> 116 us
  Pallas kernels: 28.4 us -> 12.5 us
    pallas_call x2, Pallas kernels: 28.4 us -> 12.5 us  [tile_products(): pl.pallas_call(kernel, grid_spec=grid_spec, out_shape=jax.ShapeDtypeStruc...]
    all_to_all x1, blocking collectives: 36.8 us -> 27.2 us  [local(): lax.all_to_all(outgoing, 'row', 0, 0, tiled=True)]
    all_to_all x1, blocking collectives: 71.8 us -> 64.9 us  [local(): received = lax.all_to_all(partial_rows, 'rep', 0, 0, tiled=True)]
where the time goes in v3:
time: 211 us; the launch traced here: 210 us
  blocking collectives  116 us (55%)
  waiting for transfers between devices  48 us (23%)
  starting transfers between devices  21.4 us (10%)
  Pallas kernels  12.5 us (6%)
  local copies, waits for them, and re-layouts  8.23 us (4%)
    all_to_all x1, blocking collectives, local(): received = lax.all_to_all(partial_rows, 'rep', 0, 0, tiled=True)  64.9 us
    all_to_all x1, waiting for transfers between devices, local(): lax.all_to_all(jnp.broadcast_to(grad_hidden[None], (rep_count, tile_size,...  27.8 us
    all_to_all x1, blocking collectives, local(): lax.all_to_all(outgoing, 'row', 0, 0, tiled=True)  27.2 us
    all_to_all x1, blocking collectives, local(): lax.all_to_all(jnp.broadcast_to(row_chunk[None], (rep_count,) + row_chunk...  23.7 us
    all_to_all x1, starting transfers between devices, local(): lax.all_to_all(jnp.broadcast_to(features[None], (row_count, tile_size, fe...  13.4 us
    pallas_call x2, Pallas kernels, tile_products(): pl.pallas_call(kernel, grid_spec=grid_spec, out_shape=jax.ShapeDtypeStruc...  12.5 us
    all_to_all x1, waiting for transfers between devices, local(): lax.all_to_all(jnp.broadcast_to(features[None], (row_count, tile_size, fe...  11.5 us
    all_to_all x1, waiting for transfers between devices, local(): lax.all_to_all(jnp.broadcast_to(rep_summed[None], (row_count,) + rep_summ...  8.69 us
  transfers between devices with their start and end apart: 3, of which 3 were waited for; matrix products, arithmetic and copies ran while one was open for 1% of the time, Pallas kernels for 0%

profile of v3, /device:TPU:1, one launch (start us, length us, event | category | flops | bytes accessed | tf_op | source)
XLA Modules:
  0.0 209.9 jit_solution(13803450019657972749)
XLA Ops:
  0.6 0.0 copy-start
  0.6 0.0 copy-start.3
  0.7 1.7 broadcast_in_dim.8
  2.3 13.4 %all-to-all-start = ((bf16[16,128,128]{2,1,0:T(8,128)(2,1)}), bf16[16,128,128]{2,1,0:T(8,128)(2,1)S(1)}, u32[]{:S(2)}, u32[]{:S(2)}) async-start(bf16[16,128,128]{2,1,0:T(8,128)(2,1)} %broadcast_in_dim.8), calls=%async_computation | async-start | bytes 1048576 | tf_op jit(solution)/shard_map/all_to_all | solution.py:85
  16.4 0.0 copy-done.3
  16.4 0.1 copy.10
  16.5 0.7 reshape_squeeze.8.coord_ref
  17.2 11.5 %all-to-all-done.source_ref = bf16[16,128,128]{2,1,0:T(8,128)(2,1)S(1)} async-done(((bf16[16,128,128]{2,1,0:T(8,128)(2,1)}), bf16[16,128,128]{2,1,0:T(8,128)(2,1)S(1)}, u32[]{:S(2)}, u32[]{:S(2)}) %all-to-all-start) | async-done | bytes 524320 | tf_op jit(solution)/shard_map/all_to_all | solution.py:85
  28.7 0.0 copy-start.2
  28.7 0.8 copy-done.2
  29.5 6.3 %shard_map.85 = f32[32,128,128]{2,1,0:T(8,128)} custom-call(s32[256]{0:T(256)} %reshape_squeeze.8.coord_ref, s32[1]{0:T(128)} %bitcast.10.live_ref, bf16[128,128,128]{2,1,0:T(8,128)(2,1)} %bitcast.12, bf16[16,128,128]{2,1,0:T(8,128)(2,1)} %copy-done.2), custom_call_target="tpu_custom_call" | custom-call | tf_op jit(solution)/shard_map/pallas_call | solution.py:68
  35.8 64.9 %all_to_all.30 = f32[32,128,128]{2,1,0:T(8,128)S(1)} all-to-all(f32[32,128,128]{2,1,0:T(8,128)} %shard_map.85), channel_id=1, replica_groups=mesh['rep'=32,'row'=16] {'rep'}, dimensions={0} | all-to-all | bytes 4194304 | tf_op jit(solution)/shard_map/all_to_all | solution.py:89
  100.7 0.0 copy-start.4
  100.7 0.1 reduce_sum.27
  100.8 0.0 copy-done
  100.8 0.7 copy-done.4
  101.5 0.8 multiply_convert_fusion
  102.4 0.2 convolution_convert_fusion
  102.5 1.2 broadcast_in_dim.9
  103.7 4.3 %all-to-all-start.2 = ((bf16[32,128,128]{2,1,0:T(8,128)(2,1)}), bf16[32,128,128]{2,1,0:T(8,128)(2,1)S(1)}, u32[]{:S(2)}, u32[]{:S(2)}) async-start(bf16[32,128,128]{2,1,0:T(8,128)(2,1)} %broadcast_in_dim.9), calls=%async_computation.2 | async-start | bytes 2097152 | tf_op jit(solution)/shard_map/all_to_all | solution.py:96
  108.1 0.2 fusion.4
  108.3 27.8 %all-to-all-done.2.source_ref = bf16[32,128,128]{2,1,0:T(8,128)(2,1)S(1)} async-done(((bf16[32,128,128]{2,1,0:T(8,128)(2,1)}), bf16[32,128,128]{2,1,0:T(8,128)(2,1)S(1)}, u32[]{:S(2)}, u32[]{:S(2)}) %all-to-all-start.2) | async-done | bytes 1048608 | tf_op jit(solution)/shard_map/all_to_all | solution.py:96
  136.1 0.0 copy-start.1
  136.1 1.0 copy-done.1
  137.1 6.2 %shard_map.86 = f32[16,128,128]{2,1,0:T(8,128)} custom-call(s32[256]{0:T(256)} %reshape_squeeze.8.coord_ref, s32[1]{0:T(128)} %bitcast.11.live_ref, bf16[128,128,128]{2,1,0:T(8,128)(2,1)} %bitcast.13, bf16[32,128,128]{2,1,0:T(8,128)(2,1)} %copy-done.1), custom_call_target="tpu_custom_call" | custom-call | tf_op jit(solution)/shard_map/pallas_call | solution.py:68
  143.2 1.3 pad_maximum_fusion
  144.6 27.2 %all_to_all.31 = f32[16,144,128]{2,1,0:T(8,128)S(1)} all-to-all(f32[16,144,128]{2,1,0:T(8,128)S(1)} %pad_maximum_fusion), channel_id=1, replica_groups=mesh['rep'=32,'row'=16] {'row'}, dimensions={0} | all-to-all | bytes 2359296 | tf_op jit(solution)/shard_map/all_to_all | solution.py:107
  171.7 0.1 reduce_sum.28
  171.8 23.7 %all_to_all.32 = f32[32,16,128]{2,1,0:T(8,128)S(1)} all-to-all(f32[32,16,128]{2,1,0:T(8,128)S(1)} %broadcast_in_dim.10), channel_id=1, replica_groups=mesh['rep'=32,'row'=16] {'rep'}, dimensions={0} | all-to-all | bytes 524288 | tf_op jit(solution)/shard_map/all_to_all | solution.py:111
  195.6 0.7 broadcast_in_dim.11
  196.2 3.7 %all-to-all-start.5 = ((f32[16,16,128]{2,1,0:T(8,128)}), f32[16,16,128]{2,1,0:T(8,128)S(1)}, u32[]{:S(2)}, u32[]{:S(2)}) async-start(f32[16,16,128]{2,1,0:T(8,128)} %broadcast_in_dim.11), calls=%async_computation.5 | async-start | bytes 262144 | tf_op jit(solution)/shard_map/all_to_all | solution.py:116
  199.9 0.6 slice.12
  200.5 8.7 %all-to-all-done.5 = f32[16,16,128]{2,1,0:T(8,128)S(1)} async-done(((f32[16,16,128]{2,1,0:T(8,128)}), f32[16,16,128]{2,1,0:T(8,128)S(1)}, u32[]{:S(2)}, u32[]{:S(2)}) %all-to-all-start.5) | async-done | bytes 131104 | tf_op jit(solution)/shard_map/all_to_all | solution.py:116
  209.2 0.7 reshape.17
  (4 shorter events, 0.1 us)
Async XLA Ops:
  0.6 100.2 %copy-start = (bf16[128,256]{1,0:T(8,128)(2,1)S(1)}, bf16[128,256]{1,0:T(8,128)(2,1)}, u32[]{:S(2)}) copy-start(bf16[128,256]{1,0:T(8,128)(2,1)} %param.7) | copy-start | bytes 196612
  0.6 15.8 %copy-start.3 = (s32[1,1,128,2]{2,3,1,0:T(2,128)S(1)}, s32[1,1,128,2]{2,3,1,0:T(2,128)}, u32[]{:S(2)}) copy-start(s32[1,1,128,2]{2,3,1,0:T(2,128)} %param.10) | copy-start | bytes 3076
  2.3 26.4 %all-to-all-start = ((bf16[16,128,128]{2,1,0:T(8,128)(2,1)}), bf16[16,128,128]{2,1,0:T(8,128)(2,1)S(1)}, u32[]{:S(2)}, u32[]{:S(2)}) async-start(bf16[16,128,128]{2,1,0:T(8,128)(2,1)} %broadcast_in_dim.8), calls=%async_computation | async-start | bytes 1048576 | tf_op jit(solution)/shard_map/all_to_all | solution.py:85
  28.7 0.8 copy-start.2
  100.7 0.8 copy-start.4
  103.7 32.4 %all-to-all-start.2 = ((bf16[32,128,128]{2,1,0:T(8,128)(2,1)}), bf16[32,128,128]{2,1,0:T(8,128)(2,1)S(1)}, u32[]{:S(2)}, u32[]{:S(2)}) async-start(bf16[32,128,128]{2,1,0:T(8,128)(2,1)} %broadcast_in_dim.9), calls=%async_computation.2 | async-start | bytes 2097152 | tf_op jit(solution)/shard_map/all_to_all | solution.py:96
  136.1 1.0 copy-start.1
  196.2 13.0 %all-to-all-start.5 = ((f32[16,16,128]{2,1,0:T(8,128)}), f32[16,16,128]{2,1,0:T(8,128)S(1)}, u32[]{:S(2)}, u32[]{:S(2)}) async-start(f32[16,16,128]{2,1,0:T(8,128)} %broadcast_in_dim.11), calls=%async_computation.5 | async-start | bytes 262144 | tf_op jit(solution)/shard_map/all_to_all | solution.py:116

commit v4 on v3

--- a/solution.py
+++ b/solution.py
@@ -86,8 +86,8 @@
         jnp.broadcast_to(features[None], (row_count, tile_size, feature_size)), "row", 0, 0, tiled=True
     )
     partial_rows = tile_products(values, coords, live_count, columns, rep_count, False)
-    received = lax.all_to_all(partial_rows, "rep", 0, 0, tiled=True)
-    aggregated = jnp.sum(received, axis=0).astype(jnp.bfloat16)
+    received = lax.all_to_all(partial_rows.astype(jnp.bfloat16), "rep", 0, 0, tiled=True)
+    aggregated = jnp.sum(received.astype(jnp.float32), axis=0).astype(jnp.bfloat16)
     preactivation = jnp.dot(aggregated, weight, preferred_element_type=jnp.float32)
     grad_pre = (cotangent.astype(jnp.float32) * silu_slope(preactivation)).astype(jnp.bfloat16)
     grad_hidden = lax.dot_general(

time: 211 us -> 190 us (0.900)
  blocking collectives: 116 us -> 93.5 us
    all_to_all x1, blocking collectives: 64.9 us -> 41.6 us  [local(): lax.all_to_all(partial_rows.astype(jnp.bfloat16), 'rep', 0, 0, tiled=True)]
where the time goes in v4:
time: 190 us; the launch traced here: 189 us
  blocking collectives  93.5 us (49%)
  waiting for transfers between devices  48 us (25%)
  starting transfers between devices  21.6 us (11%)
  Pallas kernels  12.5 us (7%)
  local copies, waits for them, and re-layouts  7.52 us (4%)
  other arithmetic  3.3 us (2%)
    all_to_all x1, blocking collectives, local(): lax.all_to_all(partial_rows.astype(jnp.bfloat16), 'rep', 0, 0, tiled=True)  41.6 us
    all_to_all x1, blocking collectives, local(): lax.all_to_all(outgoing, 'row', 0, 0, tiled=True)  28.7 us
    all_to_all x1, waiting for transfers between devices, local(): lax.all_to_all(jnp.broadcast_to(grad_hidden[None], (rep_count, tile_size,...  27.8 us
    all_to_all x1, blocking collectives, local(): lax.all_to_all(jnp.broadcast_to(row_chunk[None], (rep_count,) + row_chunk...  23.3 us
    all_to_all x1, starting transfers between devices, local(): lax.all_to_all(jnp.broadcast_to(features[None], (row_count, tile_size, fe...  13.4 us
    pallas_call x2, Pallas kernels, tile_products(): pl.pallas_call(kernel, grid_spec=grid_spec, out_shape=jax.ShapeDtypeStruc...  12.5 us
    all_to_all x1, waiting for transfers between devices, local(): lax.all_to_all(jnp.broadcast_to(features[None], (row_count, tile_size, fe...  11.5 us
    all_to_all x1, waiting for transfers between devices, local(): lax.all_to_all(jnp.broadcast_to(rep_summed[None], (row_count,) + rep_summ...  8.69 us
  transfers between devices with their start and end apart: 3, of which 3 were waited for; matrix products, arithmetic and copies ran while one was open for 1% of the time, Pallas kernels for 0%

profile of v4, /device:TPU:1, one launch (start us, length us, event | category | flops | bytes accessed | tf_op | source)
XLA Modules:
  0.0 188.9 jit_solution(4801834142365421703)
XLA Ops:
  0.6 0.0 copy-start
  0.6 0.0 copy-start.3
  0.7 1.7 broadcast_in_dim.8
  2.3 13.4 %all-to-all-start = ((bf16[16,128,128]{2,1,0:T(8,128)(2,1)}), bf16[16,128,128]{2,1,0:T(8,128)(2,1)S(1)}, u32[]{:S(2)}, u32[]{:S(2)}) async-start(bf16[16,128,128]{2,1,0:T(8,128)(2,1)} %broadcast_in_dim.8), calls=%async_computation | async-start | bytes 1048576 | tf_op jit(solution)/shard_map/all_to_all | solution.py:85
  16.4 0.0 copy-done.3
  16.4 0.1 copy.10
  16.5 0.7 reshape_squeeze.8.coord_ref
  17.2 11.5 %all-to-all-done.source_ref = bf16[16,128,128]{2,1,0:T(8,128)(2,1)S(1)} async-done(((bf16[16,128,128]{2,1,0:T(8,128)(2,1)}), bf16[16,128,128]{2,1,0:T(8,128)(2,1)S(1)}, u32[]{:S(2)}, u32[]{:S(2)}) %all-to-all-start) | async-done | bytes 524320 | tf_op jit(solution)/shard_map/all_to_all | solution.py:85
  28.7 0.0 copy-start.2
  28.7 0.8 copy-done.2
  29.5 6.3 %shard_map.85 = f32[32,128,128]{2,1,0:T(8,128)} custom-call(s32[256]{0:T(256)} %reshape_squeeze.8.coord_ref, s32[1]{0:T(128)} %bitcast.10.live_ref, bf16[128,128,128]{2,1,0:T(8,128)(2,1)} %bitcast.12, bf16[16,128,128]{2,1,0:T(8,128)(2,1)} %copy-done.2), custom_call_target="tpu_custom_call" | custom-call | tf_op jit(solution)/shard_map/pallas_call | solution.py:68
  35.8 1.7 convert_element_type.18
  37.6 0.0 copy-start.4
  37.6 41.6 %all_to_all.30 = bf16[32,128,128]{2,1,0:T(8,128)(2,1)S(1)} all-to-all(bf16[32,128,128]{2,1,0:T(8,128)(2,1)S(1)} %convert_element_type.18), channel_id=1, replica_groups=mesh['rep'=32,'row'=16] {'rep'}, dimensions={0} | all-to-all | bytes 2097152 | tf_op jit(solution)/shard_map/all_to_all | solution.py:89
  79.2 0.2 reduce_sum.30
  79.3 0.0 copy-done
  79.3 0.0 copy-done.4
  79.3 0.8 multiply_convert_fusion
  80.2 0.2 convolution_convert_fusion
  80.3 1.2 broadcast_in_dim.9
  81.5 4.3 %all-to-all-start.2 = ((bf16[32,128,128]{2,1,0:T(8,128)(2,1)}), bf16[32,128,128]{2,1,0:T(8,128)(2,1)S(1)}, u32[]{:S(2)}, u32[]{:S(2)}) async-start(bf16[32,128,128]{2,1,0:T(8,128)(2,1)} %broadcast_in_dim.9), calls=%async_computation.2 | async-start | bytes 2097152 | tf_op jit(solution)/shard_map/all_to_all | solution.py:96
  85.9 0.2 fusion
  86.1 27.8 %all-to-all-done.2.source_ref = bf16[32,128,128]{2,1,0:T(8,128)(2,1)S(1)} async-done(((bf16[32,128,128]{2,1,0:T(8,128)(2,1)}), bf16[32,128,128]{2,1,0:T(8,128)(2,1)S(1)}, u32[]{:S(2)}, u32[]{:S(2)}) %all-to-all-start.2) | async-done | bytes 1048608 | tf_op jit(solution)/shard_map/all_to_all | solution.py:96
  113.9 0.0 copy-start.1
  113.9 1.0 copy-done.1
  114.8 6.2 %shard_map.86 = f32[16,128,128]{2,1,0:T(8,128)} custom-call(s32[256]{0:T(256)} %reshape_squeeze.8.coord_ref, s32[1]{0:T(128)} %bitcast.11.live_ref, bf16[128,128,128]{2,1,0:T(8,128)(2,1)} %bitcast.13, bf16[32,128,128]{2,1,0:T(8,128)(2,1)} %copy-done.1), custom_call_target="tpu_custom_call" | custom-call | tf_op jit(solution)/shard_map/pallas_call | solution.py:68
  121.0 1.3 pad_maximum_fusion
  122.3 28.7 %all_to_all.31 = f32[16,144,128]{2,1,0:T(8,128)S(1)} all-to-all(f32[16,144,128]{2,1,0:T(8,128)S(1)} %pad_maximum_fusion), channel_id=1, replica_groups=mesh['rep'=32,'row'=16] {'row'}, dimensions={0} | all-to-all | bytes 2359296 | tf_op jit(solution)/shard_map/all_to_all | solution.py:107
  151.0 0.1 reduce_sum.31
  151.1 23.3 %all_to_all.32 = f32[32,16,128]{2,1,0:T(8,128)S(1)} all-to-all(f32[32,16,128]{2,1,0:T(8,128)S(1)} %broadcast_in_dim.10), channel_id=1, replica_groups=mesh['rep'=32,'row'=16] {'rep'}, dimensions={0} | all-to-all | bytes 524288 | tf_op jit(solution)/shard_map/all_to_all | solution.py:111
  174.4 0.7 broadcast_in_dim.11
  175.1 3.8 %all-to-all-start.5 = ((f32[16,16,128]{2,1,0:T(8,128)}), f32[16,16,128]{2,1,0:T(8,128)S(1)}, u32[]{:S(2)}, u32[]{:S(2)}) async-start(f32[16,16,128]{2,1,0:T(8,128)} %broadcast_in_dim.11), calls=%async_computation.5 | async-start | bytes 262144 | tf_op jit(solution)/shard_map/all_to_all | solution.py:116
  178.9 0.6 slice.12
  179.6 8.7 %all-to-all-done.5 = f32[16,16,128]{2,1,0:T(8,128)S(1)} async-done(((f32[16,16,128]{2,1,0:T(8,128)}), f32[16,16,128]{2,1,0:T(8,128)S(1)}, u32[]{:S(2)}, u32[]{:S(2)}) %all-to-all-start.5) | async-done | bytes 131104 | tf_op jit(solution)/shard_map/all_to_all | solution.py:116
  188.2 0.7 reshape.17
  (4 shorter events, 0.1 us)
Async XLA Ops:
  0.6 78.7 %copy-start = (bf16[128,256]{1,0:T(8,128)(2,1)S(1)}, bf16[128,256]{1,0:T(8,128)(2,1)}, u32[]{:S(2)}) copy-start(bf16[128,256]{1,0:T(8,128)(2,1)} %param.7) | copy-start | bytes 196612
  0.6 15.8 %copy-start.3 = (s32[1,1,128,2]{2,3,1,0:T(2,128)S(1)}, s32[1,1,128,2]{2,3,1,0:T(2,128)}, u32[]{:S(2)}) copy-start(s32[1,1,128,2]{2,3,1,0:T(2,128)} %param.10) | copy-start | bytes 3076
  2.3 26.4 %all-to-all-start = ((bf16[16,128,128]{2,1,0:T(8,128)(2,1)}), bf16[16,128,128]{2,1,0:T(8,128)(2,1)S(1)}, u32[]{:S(2)}, u32[]{:S(2)}) async-start(bf16[16,128,128]{2,1,0:T(8,128)(2,1)} %broadcast_in_dim.8), calls=%async_computation | async-start | bytes 1048576 | tf_op jit(solution)/shard_map/all_to_all | solution.py:85
  28.7 0.8 copy-start.2
  37.6 41.8 %copy-start.4 = (bf16[128,256]{1,0:T(8,128)(2,1)S(1)}, bf16[128,256]{1,0:T(8,128)(2,1)}, u32[]{:S(2)}) copy-start(bf16[128,256]{1,0:T(8,128)(2,1)} %param.8) | copy-start | bytes 196612
  81.5 32.3 %all-to-all-start.2 = ((bf16[32,128,128]{2,1,0:T(8,128)(2,1)}), bf16[32,128,128]{2,1,0:T(8,128)(2,1)S(1)}, u32[]{:S(2)}, u32[]{:S(2)}) async-start(bf16[32,128,128]{2,1,0:T(8,128)(2,1)} %broadcast_in_dim.9), calls=%async_computation.2 | async-start | bytes 2097152 | tf_op jit(solution)/shard_map/all_to_all | solution.py:96
  113.9 1.0 copy-start.1
  175.1 13.1 %all-to-all-start.5 = ((f32[16,16,128]{2,1,0:T(8,128)}), f32[16,16,128]{2,1,0:T(8,128)S(1)}, u32[]{:S(2)}, u32[]{:S(2)}) async-start(f32[16,16,128]{2,1,0:T(8,128)} %broadcast_in_dim.11), calls=%async_computation.5 | async-start | bytes 262144 | tf_op jit(solution)/shard_map/all_to_all | solution.py:116
